TPU v7x, 512 devices: a whole 4x4x16 slice. The times are simulated.
512 devices in a mesh: tok: 16 (over z), head: 32 (over y, x, core).
Axes of the slice: x: 4, y: 4, z: 16, core: 2. Of those that a mesh axis runs over, the one named last changes fastest.
Arguments:
- tokens: bfloat16 [3072, 4096], P(('tok', 'head')), may hold values from -6 to 6
- ln1_gain: float32 [4096], replicated, may hold values from 0.25 to 1.75
- ln1_bias: float32 [4096], replicated, may hold values from -1.75 to 1.75
- ln2_gain: float32 [4096], replicated, may hold values from 0.25 to 1.75
- ln2_bias: float32 [4096], replicated, may hold values from -1.75 to 1.75
- w_qkv: bfloat16 [4096, 12288], P('tok', 'head'), may hold values from -0.09375 to 0.09375
- b_qkv: float32 [12288], P('head'), may hold values from -3 to 3
- w_dense: bfloat16 [4096, 4096], P('head', 'tok'), may hold values from -0.09375 to 0.09375
- b_dense: float32 [4096], replicated, may hold values from -1.75 to 1.75
- w_up: bfloat16 [4096, 16384], P('tok', 'head'), may hold values from -0.09375 to 0.09375
- b_up: float32 [16384], P('head'), may hold values from -3 to 3
- w_down: bfloat16 [16384, 4096], P('head', 'tok'), may hold values from -0.046875 to 0.046875
- b_down: float32 [4096], replicated, may hold values from -1.75 to 1.75
- k_cache: bfloat16 [98304, 4096], P('tok', 'head'), may hold values from -610 to 610
- v_cache: bfloat16 [98304, 4096], P('tok', 'head'), may hold values from -6 to 6
- cache_lengths: int32 [16, 33], P('tok'), may hold values from 1 to 4096, 6144 in all within a row
Outputs:
- mixed: bfloat16 [3072, 4096], P(('tok', 'head'))
Inputs may be any that keep to these rules, and one draw needn't show every extreme that they name: `cache_lengths`: row g lists the cache lengths of group g's 33 requests in the order in which their caches lie in the group's 6144 cache rows; every row sums to 6144. Request 0 of a group is the one whose 160 new tokens are prefilled, the others decode one token each.
All inputs are finite; a program needn't handle non-finite values.
Results may differ from a plain program's by a relative error of at most 0.02.
Values may be sent and summed in bfloat16 or wider, within the bound.
No kernel may reach another device: no remote copies, remote signals or barrier semaphores. Data moves between devices by JAX's collectives and lax.ppermute only.
A program may use at most 64 MiB of HBM per device.

v0:
```python
import jax
import jax.numpy as jnp
from jax import lax
from jax.sharding import PartitionSpec as P

HD = 128
ROT = 32
WINDOW = 2048
SINKS = 4
epsilon = 1e-05


def layer_norm(values, gain, shift):
    values = values.astype(jnp.float32)
    center = jnp.mean(values, axis=-1, keepdims=True)
    spread = jnp.mean(jnp.square(values - center), axis=-1, keepdims=True)
    return (values - center) * lax.rsqrt(spread + epsilon) * gain + shift


def rotate(values, positions):
    half = ROT // 2
    inverse = jnp.power(jnp.float32(10000.0), -jnp.arange(half, dtype=jnp.float32) * (2.0 / ROT))
    angles = (
        positions.astype(jnp.float32).reshape(positions.shape + (1,) * (values.ndim - 1)) * inverse
    )
    cosine = jnp.cos(angles)
    sine = jnp.sin(angles)
    first = values[..., :half]
    second = values[..., half:ROT]
    rest = values[..., ROT:]
    return jnp.concatenate(
        [first * cosine - second * sine, second * cosine + first * sine, rest], axis=-1
    )


def token_layout(lengths_row, group_rows):
    requests_count = lengths_row.shape[0]
    count_pre = group_rows - (requests_count - 1)
    index = jnp.arange(group_rows, dtype=jnp.int32)
    owner = jnp.maximum(index - (count_pre - 1), 0)
    table = owner[:, None] == jnp.arange(requests_count, dtype=jnp.int32)[None, :]
    start = jnp.sum(jnp.where(table, lengths_row[None, :], 0), axis=1)
    place = start + jnp.where(owner == 0, index, 0)
    return (owner, place)


def slot_layout(lengths_row, slots):
    starts = jnp.cumsum(lengths_row) - lengths_row
    index = jnp.arange(slots, dtype=jnp.int32)
    inside = index[:, None] >= starts[None, :]
    owner = jnp.sum(inside.astype(jnp.int32), axis=1) - 1
    begin = jnp.max(jnp.where(inside, starts[None, :], 0), axis=1)
    return (owner, index - begin)


def visible(query_owner, query_place, key_owner, key_place):
    same = query_owner[:, None] == key_owner[None, :]
    before = key_place[None, :] <= query_place[:, None]
    near = (key_place[None, :] < SINKS) | (query_place[:, None] - key_place[None, :] < WINDOW)
    return same & before & near


def body(
    tokens,
    ln1_gain,
    ln1_bias,
    ln2_gain,
    ln2_bias,
    w_qkv,
    b_qkv,
    w_dense,
    b_dense,
    w_up,
    b_up,
    w_down,
    b_down,
    k_cache,
    v_cache,
    cache_lengths,
):
    scale = HD ** (-0.5)
    width_qkv = w_qkv.shape[1]
    width_up = w_up.shape[1]
    width_dense = w_dense.shape[0]
    packed = jnp.concatenate([w_qkv, w_up, w_dense.T, w_down.T], axis=1)
    gathered = lax.all_gather(packed, "tok", axis=0, tiled=False)
    parts = gathered.shape[0] * gathered.shape[1]
    qkv_full = gathered[:, :, :width_qkv].reshape(parts, width_qkv)
    up_full = gathered[:, :, width_qkv : width_qkv + width_up].reshape(parts, width_up)
    offset = width_qkv + width_up
    dense_t = gathered[:, :, offset : offset + width_dense].reshape(parts, width_dense)
    down_t = gathered[:, :, offset + width_dense :].reshape(parts, -1)
    whole = lax.all_gather(tokens, "head", axis=0, tiled=True)
    normed_one = layer_norm(whole, ln1_gain, ln1_bias).astype(jnp.bfloat16)
    normed_two = layer_norm(whole, ln2_gain, ln2_bias).astype(jnp.bfloat16)
    rows_total = whole.shape[0]
    projected = jnp.dot(normed_one, qkv_full, preferred_element_type=jnp.float32) + b_qkv
    upward = jnp.dot(normed_two, up_full, preferred_element_type=jnp.float32)
    lengths_row = cache_lengths[0]
    query_owner, query_place = token_layout(lengths_row, rows_total)
    queries = rotate(projected[:, :HD], query_place).astype(jnp.bfloat16)
    new_keys = rotate(projected[:, HD : 2 * HD], query_place).astype(jnp.bfloat16)
    new_values = projected[:, 2 * HD :].astype(jnp.bfloat16)
    hidden = jax.nn.gelu(upward + b_up, approximate=False).astype(jnp.bfloat16)
    slots = k_cache.shape[0]
    slot_owner, slot_place = slot_layout(lengths_row, slots)
    cache_scores = jnp.dot(queries, k_cache.T, preferred_element_type=jnp.float32) * scale
    cache_scores = jnp.where(
        visible(query_owner, query_place, slot_owner, slot_place), cache_scores, -jnp.inf
    )
    new_scores = jnp.dot(queries, new_keys.T, preferred_element_type=jnp.float32) * scale
    new_scores = jnp.where(
        visible(query_owner, query_place, query_owner, query_place), new_scores, -jnp.inf
    )
    top = jnp.maximum(jnp.max(cache_scores, axis=1), jnp.max(new_scores, axis=1))
    cache_weights = jnp.exp(cache_scores - top[:, None])
    new_weights = jnp.exp(new_scores - top[:, None])
    total = jnp.sum(cache_weights, axis=1) + jnp.sum(new_weights, axis=1)
    summed = jnp.dot(
        cache_weights.astype(jnp.bfloat16), v_cache, preferred_element_type=jnp.float32
    ) + jnp.dot(new_weights.astype(jnp.bfloat16), new_values, preferred_element_type=jnp.float32)
    attention = (summed / total[:, None]).astype(jnp.bfloat16)
    contract = (((1,), (1,)), ((), ()))
    partial = lax.dot_general(
        attention, dense_t, contract, preferred_element_type=jnp.float32
    ) + lax.dot_general(hidden, down_t, contract, preferred_element_type=jnp.float32)
    heads = lax.axis_size("head")
    partial = partial.astype(jnp.bfloat16).reshape(heads, rows_total // heads, -1)
    partial_value = lax.psum_scatter(partial, "head", scatter_dimension=0, tiled=True)
    partial_value = partial_value.reshape(tokens.shape).astype(jnp.float32)
    mixed = tokens.astype(jnp.float32) + partial_value + b_dense + b_down
    return mixed.astype(jnp.bfloat16)


def solution(mesh):
    placed = (
        P(("tok", "head"), None),
        P(),
        P(),
        P(),
        P(),
        P("tok", "head"),
        P("head"),
        P("head", "tok"),
        P(),
        P("tok", "head"),
        P("head"),
        P("head", "tok"),
        P(),
        P("tok", "head"),
        P("tok", "head"),
        P("tok", None),
    )
    return jax.shard_map(
        body, mesh=mesh, in_specs=placed, out_specs=P(("tok", "head"), None), check_vma=False
    )
```

profile of v0, /device:TPU:2, one launch (start us, length us, event | category | flops | bytes accessed | tf_op | source)
XLA Modules:
  0.0 393.0 jit_solution(7284414699249301596)
XLA Ops:
  6.5 0.0 copy-start
  6.5 0.0 copy-start.8
  6.5 0.0 all-gather.7.cloned.1.call-start
  6.5 0.7 all-gather.7.cloned.1.call-update
  7.3 0.0 all-gather.5.cloned.1.call-start
  7.3 1.1 copy.26
  8.4 1.1 copy.25
  9.5 1.9 pad_maximum_fusion
  11.4 0.0 all-gather.5.cloned.1.call-update
  11.4 0.0 reduce-scatter.2.cloned.1.call-start
  11.4 0.0 copy-done.8
  11.4 0.2 reduce-window_clone.1
  11.7 0.1 select_reduce_fusion.1
  11.8 0.4 convert_reduce_fusion.1
  12.2 61.5 %all-gather.7.cloned.1.call-done = bf16[32,6,4096]{2,1,0:T(8,128)(2,1)} async-done(((bf16[1,6,4096]{2,1,0:T(8,128)(2,1)}), bf16[32,6,4096]{2,1,0:T(8,128)(2,1)}) %all-gather.7.cloned.1.call-update) | async-done | bytes 1572880 | tf_op jit(solution)/shard_map/all_gather | solution.py:93
  73.7 2.1 convert_reduce_fusion
  75.8 0.1 reshape.130
  75.9 3.8 reshape.127
  79.7 2.3 multiply_reduce_fusion
  82.1 163.7 %all-gather.5.cloned.1.call-done = bf16[4096,1536]{0,1:T(8,128)(2,1)} async-done(((bf16[256,1536]{0,1:T(8,128)(2,1)}), bf16[4096,1536]{0,1:T(8,128)(2,1)}) %all-gather.5.cloned.1.call-update) | async-done | bytes 12582928 | tf_op jit(solution)/shard_map/all_gather | solution.py:86
  245.7 7.9 %copy.29 = bf16[192,8,16,256]{3,2,1,0:T(8,128)(2,1)S(1)} copy(bf16[192,8,16,256]{3,1,2,0:T(8,128)(2,1)} %bitcast.40) | data formatting | bytes 25165824
  253.7 0.1 slice.63
  253.8 0.2 slice.55
  254.0 0.0 copy-start.3
  254.0 0.0 copy-start.9
  254.0 0.0 copy-start.10
  254.0 0.0 copy-start.13
  254.0 1.6 copy.30
  255.6 0.3 copy-done.3
  255.9 0.0 copy-done.9
  255.9 0.0 copy-done.10
  255.9 0.0 copy-done.13
  255.9 1.2 fusion.144
  257.1 0.1 fusion.101
  257.2 0.3 fusion.146
  257.5 0.0 copy-done
  257.5 2.7 fusion.145
  260.2 0.2 fusion.82
  260.4 0.1 fusion.77
  260.5 0.8 fusion.142
  261.3 0.4 copy.31
  261.7 0.6 copy-done.2
  262.3 0.8 fusion.4
  263.1 4.3 %copy.33 = bf16[64,8,16,256]{3,1,2,0:T(8,128)(2,1)} copy(bf16[64,8,16,256]{3,2,1,0:T(8,128)(2,1)S(1)} %bitcast.39) | data formatting | bytes 8388608
  267.4 4.3 %copy.32 = bf16[64,8,16,256]{3,1,2,0:T(8,128)(2,1)} copy(bf16[64,8,16,256]{3,2,1,0:T(8,128)(2,1)S(1)} %bitcast.38) | data formatting | bytes 8388608
  271.7 0.0 copy-done.4
  271.7 0.0 copy-start.14
  271.7 5.4 %fusion.32 = f32[192,4096]{1,0:T(8,128)} fusion(bf16[4096,128]{0,1:T(8,128)(2,1)S(1)} %bitcast.42, f32[192,128]{1,0:T(8,128)S(1)} %fusion.82, bf16[6144,128]{1,0:T(8,128)(2,1)S(1)} %copy-done.4, f32[192,6144]{1,0:T(8,128)} %copy-done.2, f32[192]{0:T(256)S(1)} %max.37, f32[192]{0:T(256)S(1)} %add.133), kind=kOutput, calls=%fused_computation.32 | convolution fusion | flops 505749504 | bytes 10585600 | tf_op jit(solution)/shard_map/dot_general | solution.py:124
  277.1 0.0 copy-done.11
  277.1 0.0 copy-done.12
  277.1 0.0 copy-done.14
  277.1 0.0 copy-start.1
  277.1 8.7 %fusion.1 = bf16[192,4096]{1,0:T(8,128)(2,1)S(1)} fusion(f32[192,4096]{1,0:T(8,128)} %fusion.32, bf16[4096,512]{0,1:T(8,128)(2,1)} %bitcast.43, bf16[4096,512]{0,1:T(8,128)(2,1)} %bitcast.44, f32[192,4096]{1,0:T(8,128)} %reshape.127, f32[4096]{0:T(1024)S(1)} %copy-done.11, f32[4096]{0:T(1024)S(1)} %copy-done.12, f32[192]{0:T(256)S(1)} %add_rsqrt_fusion, ...), kind=kOutput, calls=%fused_computation.3 | convolution fusion | flops 1622605824 | bytes 16289280 | tf_op jit(solution)/shard_map/dot_general | solution.py:126
  285.8 0.0 copy-start.5
  285.8 0.0 copy-start.6
  285.8 0.0 copy-start.7
  285.8 1.6 reshape.122
  287.5 0.0 reduce-scatter.2.cloned.1.call-update
  287.5 97.5 %reduce-scatter.2.cloned.1.call-done = bf16[1,6,4096]{2,1,0:T(8,128)(2,1)} async-done(((bf16[32,6,4096]{2,1,0:T(8,128)(2,1)}), bf16[1,6,4096]{2,1,0:T(8,128)(2,1)}) %reduce-scatter.2.cloned.1.call-update) | async-done | bytes 49168 | tf_op jit(solution)/shard_map/reduce_scatter | solution.py:129
  385.0 0.0 copy-done.5
  385.0 0.0 copy-done.6
  385.0 0.0 copy-done.7
  385.0 1.5 fusion.81
  386.5 0.0 copy-done.1
  (16 shorter events, 0.1 us)
Async XLA Ops:
  6.5 251.0 %copy-start = (bf16[6144,128]{1,0:T(8,128)(2,1)S(1)}, bf16[6144,128]{1,0:T(8,128)(2,1)}, u32[]{:S(2)}) copy-start(bf16[6144,128]{1,0:T(8,128)(2,1)} %param.29) | copy-start | bytes 4718596
  6.5 4.9 %copy-start.8 = (s32[1,33]{1,0:T(1,128)S(1)}, s32[1,33]{1,0:T(1,128)}, u32[]{:S(2)}) copy-start(s32[1,33]{1,0:T(1,128)} %param.31) | copy-start | bytes 400
  6.5 67.2 %all-gather.7.cloned.1.call-start = ((), (), s32[]{:S(2)}) async-start(), calls=%async_computation.3 | async-start | bytes 2162688 | tf_op jit(solution)/shard_map/all_gather | solution.py:93
  7.3 238.5 %all-gather.5.cloned.1.call-start = ((), (), s32[]{:S(2)}) async-start(), calls=%async_computation.2 | async-start | bytes 13369344 | tf_op jit(solution)/shard_map/all_gather | solution.py:86
  11.4 373.6 %reduce-scatter.2.cloned.1.call-start = ((), (), s32[]{:S(2)}) async-start(), calls=%async_computation.1 | async-start | bytes 2162688 | tf_op jit(solution)/shard_map/reduce_scatter | solution.py:129
  254.0 1.9 copy-start.3
  254.0 1.9 copy-start.9
  254.0 1.9 copy-start.10
  254.0 1.9 copy-start.13
  260.2 2.2 copy-start.2
  267.4 4.3 %copy-start.4 = (bf16[6144,128]{1,0:T(8,128)(2,1)S(1)}, bf16[6144,128]{1,0:T(8,128)(2,1)}, u32[]{:S(2)}) copy-start(bf16[6144,128]{1,0:T(8,128)(2,1)} %param.30) | copy-start | bytes 4718596
  271.7 5.4 %copy-start.11 = (f32[4096]{0:T(1024)S(1)}, f32[4096]{0:T(1024)}, u32[]{:S(2)}) copy-start(f32[4096]{0:T(1024)} %param.20) | copy-start | bytes 49156
  271.7 5.4 %copy-start.12 = (f32[4096]{0:T(1024)S(1)}, f32[4096]{0:T(1024)}, u32[]{:S(2)}) copy-start(f32[4096]{0:T(1024)} %param.19) | copy-start | bytes 49156
  271.7 5.4 %copy-start.14 = (f32[512]{0:T(512)S(1)}, f32[512]{0:T(512)}, u32[]{:S(2)}) copy-start(f32[512]{0:T(512)} %param.26) | copy-start | bytes 6148
  277.1 109.4 %copy-start.1 = (bf16[6144,128]{1,0:T(8,128)(2,1)S(1)}, bf16[6144,128]{1,0:T(8,128)(2,1)}, u32[]{:S(2)}) copy-start(bf16[6144,128]{1,0:T(8,128)(2,1)} %param.29) | copy-start | bytes 4718596
  285.8 99.2 %copy-start.5 = (bf16[6,4096]{1,0:T(8,128)(2,1)S(1)}, bf16[6,4096]{1,0:T(8,128)(2,1)}, u32[]{:S(2)}) copy-start(bf16[6,4096]{1,0:T(8,128)(2,1)} %param.16) | copy-start | bytes 147460
  285.8 99.2 %copy-start.6 = (f32[4096]{0:T(1024)S(1)}, f32[4096]{0:T(1024)}, u32[]{:S(2)}) copy-start(f32[4096]{0:T(1024)} %param.28) | copy-start | bytes 49156
  285.8 99.1 %copy-start.7 = (f32[4096]{0:T(1024)S(1)}, f32[4096]{0:T(1024)}, u32[]{:S(2)}) copy-start(f32[4096]{0:T(1024)} %param.24) | copy-start | bytes 49156
Sparse Core Ops, SparseCore 0:
  10.5 63.1 all-gather.6
  75.7 169.9 all-gather.4
  287.6 97.3 reduce-scatter.1
where the time goes:
time: 393 us
  waiting for transfers between devices  323 us (82%)
  local copies, waits for them, and re-layouts  28.1 us (7%)
  matrix products  18.4 us (5%)
  between operations  13.4 us (3%)
  other arithmetic  9.59 us (2%)
    all_gather x1, waiting for transfers between devices, body(): gathered = lax.all_gather(packed, 'tok', axis=0, tiled=False)  164 us
    reduce_scatter x1, waiting for transfers between devices, body(): lax.psum_scatter(partial, 'head', scatter_dimension=0, tiled=True)  97.5 us
    all_gather x1, waiting for transfers between devices, body(): whole = lax.all_gather(tokens, 'head', axis=0, tiled=True)  61.5 us
    unnamed x37, local copies, waits for them, and re-layouts  21.5 us
    dot_general x1, matrix products, body(): lax.dot_general(hidden, down_t, contract, preferred_element_type=jnp.floa...  8.67 us
  transfers between devices with their start and end apart: 3, of which 3 were waited for; matrix products, arithmetic and copies ran while one was open for 3% of the time, Pallas kernels for 0%

commit v1 on v0

--- a/solution.py
+++ b/solution.py
@@ -90,7 +90,10 @@
     offset = width_qkv + width_up
     dense_t = gathered[:, :, offset : offset + width_dense].reshape(parts, width_dense)
     down_t = gathered[:, :, offset + width_dense :].reshape(parts, -1)
-    whole = lax.all_gather(tokens, "head", axis=0, tiled=True)
+    n_dev = lax.axis_size("head")
+    tiles = jnp.stack([tokens for _ in range(n_dev)])
+    tiles = lax.all_to_all(tiles, "head", split_axis=0, concat_axis=0)
+    whole = jnp.concatenate(tiles, axis=0)
     normed_one = layer_norm(whole, ln1_gain, ln1_bias).astype(jnp.bfloat16)
     normed_two = layer_norm(whole, ln2_gain, ln2_bias).astype(jnp.bfloat16)
     rows_total = whole.shape[0]

time: 393 us -> 336 us (0.85)
  waiting for transfers between devices: 323 us -> 243 us
  starting transfers between devices: 0.08 us -> 10.4 us
  local copies, waits for them, and re-layouts: 28.1 us -> 34.5 us
  other arithmetic: 9.59 us -> 14.9 us
    all_gather x1 -> x0, waiting for transfers between devices: 61.5 us -> none  [body(): whole = lax.all_gather(tokens, 'head', axis=0, tiled=True)]
    all_gather x1, waiting for transfers between devices: 164 us -> 118 us  [body(): gathered = lax.all_gather(packed, 'tok', axis=0, tiled=False)]
    all_to_all x0 -> x1, waiting for transfers between devices: none -> 27.2 us  [body(): tiles = lax.all_to_all(tiles, 'head', split_axis=0, concat_axis=0)]
    all_to_all x0 -> x1, starting transfers between devices: none -> 10.4 us  [body(): tiles = lax.all_to_all(tiles, 'head', split_axis=0, concat_axis=0)]
    convert_element_type x0 -> x1, other arithmetic: none -> 5.18 us  [body(): normed_two = layer_norm(whole, ln2_gain, ln2_bias).astype(jnp.bfloat16)]
    unnamed x37 -> x35, local copies, waits for them, and re-layouts: 21.5 us -> 21.3 us
  transfers between devices with their start and end apart: 3 -> 3, of which waited for: 3 -> 3; matrix products, arithmetic and copies ran while one was open for 3% -> 6% of each run, Pallas kernels for 0% -> 0%
where the time goes in v1:
time: 336 us; the launch traced here: 335 us
  waiting for transfers between devices  243 us (72%)
  local copies, waits for them, and re-layouts  34.5 us (10%)
  matrix products  18.9 us (6%)
  other arithmetic  14.9 us (4%)
  between operations  13.7 us (4%)
  starting transfers between devices  10.4 us (3%)
    all_gather x1, waiting for transfers between devices, body(): gathered = lax.all_gather(packed, 'tok', axis=0, tiled=False)  118 us
    reduce_scatter x1, waiting for transfers between devices, body(): lax.psum_scatter(partial, 'head', scatter_dimension=0, tiled=True)  97.5 us
    all_to_all x1, waiting for transfers between devices, body(): tiles = lax.all_to_all(tiles, 'head', split_axis=0, concat_axis=0)  27.2 us
    unnamed x35, local copies, waits for them, and re-layouts  21.3 us
    all_to_all x1, starting transfers between devices, body(): tiles = lax.all_to_all(tiles, 'head', split_axis=0, concat_axis=0)  10.4 us
    dot_general x1, matrix products, body(): lax.dot_general(hidden, down_t, contract, preferred_element_type=jnp.floa...  8.91 us
  transfers between devices with their start and end apart: 3, of which 3 were waited for; matrix products, arithmetic and copies ran while one was open for 6% of the time, Pallas kernels for 0%

profile of v1, /device:TPU:2, one launch (start us, length us, event | category | flops | bytes accessed | tf_op | source)
XLA Modules:
  0.0 335.1 jit_solution(15912548047222850350)
XLA Ops:
  6.5 0.0 copy-start
  6.5 0.0 all-gather.3.cloned.1.call-start
  6.5 1.2 copy.24
  7.7 1.1 copy.23
  8.8 0.0 copy-start.11
  8.8 1.9 pad_maximum_fusion
  10.7 0.0 all-gather.3.cloned.1.call-update
  10.8 2.4 stack.2
  13.2 0.0 copy-start.5
  13.2 0.0 copy-start.6
  13.2 0.0 copy-start.7
  13.2 0.0 copy-start.8
  13.2 10.4 %all-to-all-start = ((bf16[32,6,4096]{2,1,0:T(8,128)(2,1)}), bf16[32,6,4096]{2,1,0:T(8,128)(2,1)}, u32[]{:S(2)}, u32[]{:S(2)}) async-start(bf16[32,6,4096]{2,1,0:T(8,128)(2,1)} %stack.2), calls=%async_computation | async-start | bytes 4194304 | tf_op jit(solution)/shard_map/all_to_all | solution.py:95
  23.6 0.0 reduce-scatter.2.cloned.1.call-start
  23.7 0.0 copy-done.11
  23.7 0.2 reduce-window_clone.1
  23.9 0.1 select_reduce_fusion.1
  24.0 0.4 convert_reduce_fusion.1
  24.4 27.2 %all-to-all-done = bf16[32,6,4096]{2,1,0:T(8,128)(2,1)} async-done(((bf16[32,6,4096]{2,1,0:T(8,128)(2,1)}), bf16[32,6,4096]{2,1,0:T(8,128)(2,1)}, u32[]{:S(2)}, u32[]{:S(2)}) %all-to-all-start) | async-done | bytes 1572896 | tf_op jit(solution)/shard_map/all_to_all | solution.py:95
  51.6 2.1 convert_reduce_fusion
  53.7 2.4 fusion.12
  56.1 0.0 copy-done.5
  56.1 0.0 copy-done.6
  56.2 0.0 copy-done.7
  56.2 0.0 copy-done.8
  56.2 5.2 %fusion.11 = (bf16[32,6,4096]{2,1,0:T(8,128)(2,1)}, bf16[32,6,4096]{2,1,0:T(8,128)(2,1)}) fusion(bf16[32,6,4096]{2,1,0:T(8,128)(2,1)} %all-to-all-done, f32[4096]{0:T(1024)S(1)} %copy-done.5, f32[4096]{0:T(1024)S(1)} %copy-done.6, f32[32,6]{1,0:T(8,128)S(1)} %add_rsqrt_fusion, f32[32,6]{1,0:T(8,128)S(1)} %broadcast_multiply_fusion, f32[4096]{0:T(1024)S(1)} %copy-done.7, ...), kind=kLoop, calls=%fused_computation.17 | loop fusion | flops 7077888 | bytes 4785664 | tf_op jit(solution)/shard_map/convert_element_type | solution.py:98
  61.4 3.6 %convert_element_type.65 = bf16[192,4096]{1,0:T(8,128)(2,1)} reshape(bf16[32,6,4096]{2,1,0:T(8,128)(2,1)} %get-tuple-element.10) | data formatting | bytes 3145728 | tf_op jit(solution)/shard_map/convert_element_type | solution.py:97
  65.0 2.6 convert_element_type.71
  67.6 118.0 %all-gather.3.cloned.1.call-done = bf16[4096,1536]{0,1:T(8,128)(2,1)} async-done(((bf16[256,1536]{0,1:T(8,128)(2,1)}), bf16[4096,1536]{0,1:T(8,128)(2,1)}) %all-gather.3.cloned.1.call-update) | async-done | bytes 12582928 | tf_op jit(solution)/shard_map/all_gather | solution.py:86
  185.6 7.9 %copy.27 = bf16[192,8,16,256]{3,2,1,0:T(8,128)(2,1)S(1)} copy(bf16[192,8,16,256]{3,1,2,0:T(8,128)(2,1)} %bitcast.41) | data formatting | bytes 25165824
  193.5 0.1 slice.63
  193.6 0.2 slice.55
  193.8 0.0 copy-start.3
  193.8 0.0 copy-start.12
  193.8 1.5 copy.28
  195.3 0.0 copy-done.3
  195.3 0.0 copy-done.12
  195.3 1.0 fusion.141
  196.3 0.1 fusion.98
  196.5 0.3 fusion.143
  196.7 0.0 copy-done
  196.7 2.7 fusion.142
  199.4 0.0 copy-start.2
  199.4 0.2 fusion.79
  199.7 0.1 fusion.74
  199.7 0.8 fusion.139
  200.5 0.4 copy.29
  201.0 0.6 copy-done.2
  201.6 0.8 fusion.13
  202.4 4.3 %copy.31 = bf16[64,8,16,256]{3,1,2,0:T(8,128)(2,1)} copy(bf16[64,8,16,256]{3,2,1,0:T(8,128)(2,1)S(1)} %bitcast.40) | data formatting | bytes 8388608
  206.7 4.2 %copy.30 = bf16[64,8,16,256]{3,1,2,0:T(8,128)(2,1)} copy(bf16[64,8,16,256]{3,2,1,0:T(8,128)(2,1)S(1)} %bitcast.39) | data formatting | bytes 8388608
  210.9 0.0 copy-start.13
  210.9 5.9 %fusion.29 = f32[192,4096]{1,0:T(8,128)} fusion(bf16[4096,128]{0,1:T(8,128)(2,1)S(1)} %bitcast.43, f32[192,128]{1,0:T(8,128)S(1)} %fusion.79, bf16[6144,128]{1,0:T(8,128)(2,1)} %param.30, f32[192,6144]{1,0:T(8,128)} %copy-done.2, f32[192]{0:T(256)S(1)} %max.37, f32[192]{0:T(256)S(1)} %add.135), kind=kOutput, calls=%fused_computation.30 | convolution fusion | flops 505749504 | bytes 10585600 | tf_op jit(solution)/shard_map/dot_general | solution.py:127
  216.8 0.0 copy-done.13
  216.8 0.0 copy-start.1
  216.8 8.9 %fusion.1 = bf16[192,4096]{1,0:T(8,128)(2,1)} fusion(f32[192,4096]{1,0:T(8,128)} %fusion.29, bf16[4096,512]{0,1:T(8,128)(2,1)} %bitcast.44, bf16[192,4096]{1,0:T(8,128)(2,1)S(1)} %convert_element_type.71, bf16[4096,512]{0,1:T(8,128)(2,1)} %bitcast.45, f32[512]{0:T(512)S(1)} %copy-done.13), kind=kOutput, calls=%fused_computation.5 | convolution fusion | flops 1618673664 | bytes 14682112 | tf_op jit(solution)/shard_map/dot_general | solution.py:129
  225.7 3.5 %reshape.178 = bf16[32,6,4096]{2,1,0:T(8,128)(2,1)} reshape(bf16[192,4096]{1,0:T(8,128)(2,1)} %fusion.1) | data formatting | bytes 3145728 | tf_op jit(solution)/shard_map/reshape | solution.py:131
  229.2 0.0 reduce-scatter.2.cloned.1.call-update
  229.3 97.5 %reduce-scatter.2.cloned.1.call-done = bf16[1,6,4096]{2,1,0:T(8,128)(2,1)} async-done(((bf16[32,6,4096]{2,1,0:T(8,128)(2,1)}), bf16[1,6,4096]{2,1,0:T(8,128)(2,1)}) %reduce-scatter.2.cloned.1.call-update) | async-done | bytes 49168 | tf_op jit(solution)/shard_map/reduce_scatter | solution.py:132
  326.7 0.0 copy-done.4
  326.7 0.0 copy-done.9
  326.7 0.0 copy-done.10
  326.7 1.5 fusion.78
  328.2 0.0 copy-done.1
  (15 shorter events, 0.1 us)
Async XLA Ops:
  6.5 190.2 %copy-start = (bf16[6144,128]{1,0:T(8,128)(2,1)S(1)}, bf16[6144,128]{1,0:T(8,128)(2,1)}, u32[]{:S(2)}) copy-start(bf16[6144,128]{1,0:T(8,128)(2,1)} %param.29) | copy-start | bytes 4718596
  6.5 179.0 %all-gather.3.cloned.1.call-start = ((), (), s32[]{:S(2)}) async-start(), calls=%async_computation.3 | async-start | bytes 13369344 | tf_op jit(solution)/shard_map/all_gather | solution.py:86
  8.8 14.9 %copy-start.11 = (s32[1,33]{1,0:T(1,128)S(1)}, s32[1,33]{1,0:T(1,128)}, u32[]{:S(2)}) copy-start(s32[1,33]{1,0:T(1,128)} %param.31) | copy-start | bytes 400
  13.2 43.0 %copy-start.5 = (f32[4096]{0:T(1024)S(1)}, f32[4096]{0:T(1024)}, u32[]{:S(2)}) copy-start(f32[4096]{0:T(1024)} %param.20) | copy-start | bytes 49156
  13.2 43.0 %copy-start.6 = (f32[4096]{0:T(1024)S(1)}, f32[4096]{0:T(1024)}, u32[]{:S(2)}) copy-start(f32[4096]{0:T(1024)} %param.19) | copy-start | bytes 49156
  13.2 43.0 %copy-start.7 = (f32[4096]{0:T(1024)S(1)}, f32[4096]{0:T(1024)}, u32[]{:S(2)}) copy-start(f32[4096]{0:T(1024)} %param.18) | copy-start | bytes 49156
  13.2 43.0 %copy-start.8 = (f32[4096]{0:T(1024)S(1)}, f32[4096]{0:T(1024)}, u32[]{:S(2)}) copy-start(f32[4096]{0:T(1024)} %param.17) | copy-start | bytes 49156
  13.2 38.4 %all-to-all-start = ((bf16[32,6,4096]{2,1,0:T(8,128)(2,1)}), bf16[32,6,4096]{2,1,0:T(8,128)(2,1)}, u32[]{:S(2)}, u32[]{:S(2)}) async-start(bf16[32,6,4096]{2,1,0:T(8,128)(2,1)} %stack.2), calls=%async_computation | async-start | bytes 4194304 | tf_op jit(solution)/shard_map/all_to_all | solution.py:95
  23.6 303.1 %reduce-scatter.2.cloned.1.call-start = ((), (), s32[]{:S(2)}) async-start(), calls=%async_computation.2 | async-start | bytes 2162688 | tf_op jit(solution)/shard_map/reduce_scatter | solution.py:132
  193.8 1.5 copy-start.3
  193.8 1.5 copy-start.12
  199.4 2.2 copy-start.2
  210.9 5.9 %copy-start.13 = (f32[512]{0:T(512)S(1)}, f32[512]{0:T(512)}, u32[]{:S(2)}) copy-start(f32[512]{0:T(512)} %param.26) | copy-start | bytes 6148
  216.8 111.5 %copy-start.1 = (bf16[6144,128]{1,0:T(8,128)(2,1)S(1)}, bf16[6144,128]{1,0:T(8,128)(2,1)}, u32[]{:S(2)}) copy-start(bf16[6144,128]{1,0:T(8,128)(2,1)} %param.29) | copy-start | bytes 4718596
  225.7 101.1 %copy-start.4 = (bf16[6,4096]{1,0:T(8,128)(2,1)S(1)}, bf16[6,4096]{1,0:T(8,128)(2,1)}, u32[]{:S(2)}) copy-start(bf16[6,4096]{1,0:T(8,128)(2,1)} %param.16) | copy-start | bytes 147460
  225.7 101.1 %copy-start.9 = (f32[4096]{0:T(1024)S(1)}, f32[4096]{0:T(1024)}, u32[]{:S(2)}) copy-start(f32[4096]{0:T(1024)} %param.28) | copy-start | bytes 49156
  225.7 101.1 %copy-start.10 = (f32[4096]{0:T(1024)S(1)}, f32[4096]{0:T(1024)}, u32[]{:S(2)}) copy-start(f32[4096]{0:T(1024)} %param.24) | copy-start | bytes 49156
Sparse Core Ops, SparseCore 0:
  10.9 174.6 all-gather.2
  229.4 97.3 reduce-scatter.1
